TPU v7x, 32 devices: a whole 2x2x4 slice. The times are simulated.
32 devices in a mesh: grp: 2 (over x), gx: 16 (over z, y, core).
Axes of the slice: x: 2, y: 2, z: 4, core: 2. Of those that a mesh axis runs over, the one named last changes fastest.
Arguments:
- e_forward: float32 [3, 256, 32, 256], P(None, ('grp', 'gx')), parts along dimension 1, may hold values from -6 to 6
- h_forward: float32 [3, 256, 32, 256], P(None, ('grp', 'gx')), parts along dimension 1, may hold values from -6 to 6
- p_forward: float32 [3, 256, 32, 256], P(None, ('grp', 'gx')), parts along dimension 1, may hold values from -6 to 6
- j_forward: float32 [3, 256, 32, 256], P(None, ('grp', 'gx')), parts along dimension 1, may hold values from -6 to 6
- e_adjoint: float32 [3, 256, 32, 256], P(None, ('grp', 'gx')), parts along dimension 1, may hold values from -6 to 6
- h_adjoint: float32 [3, 256, 32, 256], P(None, ('grp', 'gx')), parts along dimension 1, may hold values from -6 to 6
- p_adjoint: float32 [3, 256, 32, 256], P(None, ('grp', 'gx')), parts along dimension 1, may hold values from -6 to 6
- j_adjoint: float32 [3, 256, 32, 256], P(None, ('grp', 'gx')), parts along dimension 1, may hold values from -6 to 6
- design: float32 [32, 32, 256], P(('grp', 'gx')), parts along dimension 0, may hold values from 0 to 1
- source_amp: float32 [32, 3], P('grp'), parts along dimension 0, may hold values from -6 to 6
- source_cell: int32 [32], P('grp'), parts along dimension 0, may hold values from 0 to 1048575
- monitor_cell: int32 [32], P('grp'), parts along dimension 0, may hold values from 0 to 1048575
- slab_start: int32 [2], P('grp'), parts along dimension 0, may hold values from 8 to 15
- radius: int32 [2], P('grp'), parts along dimension 0, may hold values from 1 to 4
Outputs:
- e_forward_next: float32 [3, 256, 32, 256], P(None, ('grp', 'gx')), parts along dimension 1
- h_forward_next: float32 [3, 256, 32, 256], P(None, ('grp', 'gx')), parts along dimension 1
- e_adjoint_next: float32 [3, 256, 32, 256], P(None, ('grp', 'gx')), parts along dimension 1
- h_adjoint_next: float32 [3, 256, 32, 256], P(None, ('grp', 'gx')), parts along dimension 1
- design_grad: float32 [32, 32, 256], P(('grp', 'gx')), parts along dimension 0
There are 2 independent parts, one for each index of `grp`. A program takes and returns all parts, laid end to end along the dimension named above; each array names one. Nothing has to cross between parts.
Inputs may be any that keep to these rules, and one draw needn't show every extreme that they name: `slab_start`: the slab begins within planes 8 to 15 of the grid.
All inputs are finite; a program needn't handle non-finite values.
Results may differ from a plain program's by a relative error of at most 0.0003.
Values sent between devices are 32-bit elements; how exact they have to be, the bound alone decides.
No kernel may reach another device: no remote copies, remote signals or barrier semaphores. Data moves between devices by JAX's collectives and lax.ppermute only.
A program may use at most 128 MiB of HBM per device.

v0:
```python
import jax
import jax.numpy as jnp
from jax import lax
from jax.sharding import PartitionSpec as P

DT = 0.5
EPS_RANGE = 10.0
STRENGTH_BASE = 0.5
STRENGTH_RANGE = 3.0
DAMPING = 0.2
GAIN_FIELD = 0.25
HIGH = lax.Precision.HIGHEST


def passed_along(block, axis, distance):
    devices = range(lax.axis_size(axis))
    route = [(i - distance, i) for i in devices if i - distance in devices]
    return lax.ppermute(block, axis, route)


def band_matrix(count, radius):
    rows = jnp.arange(count, dtype=jnp.int32)
    dist = jnp.abs(rows[:, None] - rows[None, :])
    weights = jnp.maximum(radius + 1 - dist, 0).astype(jnp.float32)
    return weights / jnp.sum(weights, axis=1, keepdims=True)


def ahead(field, axis):
    count = field.shape[axis]
    rest = lax.slice_in_dim(field, 1, count, axis=axis)
    return jnp.concatenate([rest, jnp.zeros_like(lax.slice_in_dim(field, 0, 1, axis=axis))], axis)


def behind(field, axis):
    count = field.shape[axis]
    rest = lax.slice_in_dim(field, 0, count - 1, axis=axis)
    return jnp.concatenate([jnp.zeros_like(lax.slice_in_dim(field, 0, 1, axis=axis)), rest], axis)


def update_h(efield, hfield, upper):
    ex, ey, ez = (efield[0], efield[1], efield[2])
    ex_next = jnp.concatenate([ex[1:], upper[0][None]], 0)
    ey_next = jnp.concatenate([ey[1:], upper[1][None]], 0)
    curl_x = ahead(ez, 2) - ez - (ey_next - ey)
    curl_y = ex_next - ex - (ahead(ez, 1) - ez)
    curl_z = ahead(ey, 1) - ey - (ahead(ex, 2) - ex)
    return hfield - DT * jnp.stack([curl_x, curl_y, curl_z])


def update_e(efield, hnext, lower, jnext, permittivity, drive):
    hx, hy, hz = (hnext[0], hnext[1], hnext[2])
    hx_prev = jnp.concatenate([lower[0][None], hx[:-1]], 0)
    hy_prev = jnp.concatenate([lower[1][None], hy[:-1]], 0)
    curl_x = hz - behind(hz, 2) - (hy - hy_prev)
    curl_y = hx - hx_prev - (hz - behind(hz, 1))
    curl_z = hy - behind(hy, 1) - (hx - behind(hx, 2))
    curl = jnp.stack([curl_x, curl_y, curl_z])
    return efield + (DT / permittivity)[None] * (curl - jnext + drive)


def update_j(jfield, pfield, efield, strength):
    return ((1.0 - DAMPING * DT / 2.0) * jfield + DT * (strength[None] * efield - pfield)) / (
        1.0 + DAMPING * DT / 2.0
    )


def smooth(wx, wy, planes):
    inner = jnp.einsum("ax,zxy->zay", wx, planes, precision=HIGH)
    return jnp.einsum("zay,by->zab", inner, wy, precision=HIGH)


def smooth_adjoint(wx, wy, planes):
    inner = jnp.einsum("ax,zab->zxb", wx, planes, precision=HIGH)
    return jnp.einsum("zxb,by->zxy", inner, wy, precision=HIGH)


def locate(cells, first, depth, width_x, width_y):
    zz = cells // (width_x * width_y)
    rest = cells % (width_x * width_y)
    local = zz - first
    inside = ((local >= 0) & (local < depth)).astype(jnp.float32)
    return (jnp.clip(local, 0, depth - 1), rest // width_y, rest % width_y, inside)


def body(
    e_forward,
    h_forward,
    p_forward,
    j_forward,
    e_adjoint,
    h_adjoint,
    p_adjoint,
    j_adjoint,
    design,
    source_amp,
    source_cell,
    monitor_cell,
    slab_start,
    radius,
):
    index = lax.axis_index("gx")
    depth, width_x, width_y = (e_forward.shape[1], e_forward.shape[2], e_forward.shape[3])
    start = slab_start[0]
    wx = band_matrix(width_x, radius[0])
    wy = band_matrix(width_y, radius[0])
    upper = passed_along(
        jnp.stack([e_forward[0, 0], e_forward[1, 0], e_adjoint[0, 0], e_adjoint[1, 0]]), "gx", -1
    )
    hf = update_h(e_forward, h_forward, upper[0:2])
    ha = update_h(e_adjoint, h_adjoint, upper[2:4])
    gathered = lax.all_gather(design, "gx", axis=0, tiled=True)
    slab = gathered.shape[0]
    planes = index * depth + jnp.arange(depth, dtype=jnp.int32) - start
    valid = ((planes >= 0) & (planes < slab)).astype(jnp.float32)
    picked = jnp.take(gathered, jnp.clip(planes, 0, slab - 1), axis=0) * valid[:, None, None]
    density = smooth(wx, wy, picked)
    permittivity = 1.0 + EPS_RANGE * density
    strength = STRENGTH_BASE + STRENGTH_RANGE * density
    lower = passed_along(jnp.stack([hf[0, -1], hf[1, -1], ha[0, -1], ha[1, -1]]), "gx", 1)
    zs, xs, ys, inside_s = locate(source_cell, index * depth, depth, width_x, width_y)
    nsrc = zs.shape[0]
    comp = jnp.repeat(jnp.arange(3, dtype=jnp.int32), nsrc)
    drive = (
        jnp.zeros((3, depth, width_x, width_y), jnp.float32)
        .at[comp, jnp.tile(zs, 3), jnp.tile(xs, 3), jnp.tile(ys, 3)]
        .add((source_amp.T * inside_s[None, :]).reshape(-1))
    )
    zm, xm, ym, inside_m = locate(monitor_cell, index * depth, depth, width_x, width_y)
    count = jnp.zeros((depth, width_x, width_y), jnp.float32).at[zm, xm, ym].add(inside_m)
    drive_adj = count[None] * e_forward
    jf = update_j(j_forward, p_forward, e_forward, strength)
    ja = update_j(j_adjoint, p_adjoint, e_adjoint, strength)
    ef = update_e(e_forward, hf, lower[0:2], jf, permittivity, drive)
    ea = update_e(e_adjoint, ha, lower[2:4], ja, permittivity, drive_adj)
    intersection = jnp.sum(ea * (ef - e_forward + GAIN_FIELD * ef), axis=0)
    slots = jnp.arange(slab, dtype=jnp.int32)
    select = (planes[:, None] == slots[None, :]).astype(jnp.float32)
    returned = jnp.einsum("lo,lxy->oxy", select, intersection, precision=HIGH)
    own_intersection = lax.psum_scatter(returned, "gx", scatter_dimension=0, tiled=True)
    design_grad = smooth_adjoint(wx, wy, own_intersection)
    return (ef, hf, ea, ha, design_grad)


def solution(mesh):
    return jax.shard_map(
        body,
        mesh=mesh,
        in_specs=(
            P(None, ("grp", "gx"), None, None),
            P(None, ("grp", "gx"), None, None),
            P(None, ("grp", "gx"), None, None),
            P(None, ("grp", "gx"), None, None),
            P(None, ("grp", "gx"), None, None),
            P(None, ("grp", "gx"), None, None),
            P(None, ("grp", "gx"), None, None),
            P(None, ("grp", "gx"), None, None),
            P(("grp", "gx"), None, None),
            P("grp", None),
            P("grp"),
            P("grp"),
            P("grp"),
            P("grp"),
        ),
        out_specs=(
            P(None, ("grp", "gx"), None, None),
            P(None, ("grp", "gx"), None, None),
            P(None, ("grp", "gx"), None, None),
            P(None, ("grp", "gx"), None, None),
            P(("grp", "gx"), None, None),
        ),
        check_vma=False,
    )
```

profile of v0, /device:TPU:0, one launch (start us, length us, event | category | flops | bytes accessed | tf_op | source)
XLA Modules:
  0.0 142.5 jit_solution(9310592674110908171)
XLA Ops:
  7.2 0.9 slice_bitcast_fusion.25
  8.1 0.7 pad_maximum_fusion
  8.8 1.3 collective-permute-start
  10.7 0.7 convert_reduce_fusion.1
  11.4 0.7 convert_reduce_fusion
  12.1 1.9 %slice_bitcast_fusion.17 = (f32[7,32,256]{2,1,0:T(8,128)}, f32[7,32,256]{2,1,0:T(8,128)}) fusion(f32[3,8,32,256]{3,2,1,0:T(8,128)} %param.18), kind=kLoop, calls=%fused_computation.73 | loop fusion | bytes 917504 | tf_op jit(solution)/shard_map/slice | solution.py:43
  14.0 0.8 slice_bitcast_fusion.19
  15.0 0.8 slice_bitcast_fusion.11
  15.8 0.7 slice.272
  16.6 0.8 slice.269
  19.7 0.7 reshape.193
  22.5 25.4 %all_gather.3 = f32[16,32,256]{2,1,0:T(8,128)S(1)} all-gather(f32[1,32,256]{2,1,0:T(8,128)} %param.22), channel_id=1, replica_groups=mesh['grp'=2,'gx'=16] {'gx'}, dimensions={0}, use_global_device_ids=true | all-gather | bytes 557056 | tf_op jit(solution)/shard_map/all_gather | solution.py:111
  47.9 0.7 slice.284
  48.7 0.8 copy-done.11
  49.6 0.8 slice.274
  50.4 0.7 slice.273
  53.1 1.3 add_divide_fusion
  54.5 1.6 %scatter_fusion.1 = f32[8,32,256]{2,1,0:T(8,128)S(1)} fusion(f32[8,32,256]{2,1,0:T(8,128)S(1)} %broadcast_in_dim.23, s32[16]{0:T(128)S(1)} %fusion.56, f32[16]{0:T(128)S(1)} %get-tuple-element.8), kind=kCustom, calls=%fused_computation.2 | custom fusion | flops 16 | bytes 384 | tf_op jit(solution)/shard_map/scatter-add | solution.py:129
  56.1 0.9 copy-done.10
  57.2 0.9 copy-done.20
  58.3 0.9 slice_bitcast_fusion.13
  59.2 0.9 slice_bitcast_fusion.2
  61.0 0.9 copy-done.21
  62.2 2.3 %collective-permute-start.1 = (f32[4,32,256]{2,1,0:T(8,128)S(1)}, f32[4,32,256]{2,1,0:T(8,128)S(1)}, u32[]{:S(2)}, u32[]{:S(2)}) collective-permute-start(f32[4,32,256]{2,1,0:T(8,128)S(1)} %pad_maximum_fusion.1), channel_id=1, source_target_pairs={{0,1},{1,2},{2,3},{3,4},{4,5},{5,6},{6,7},{7,8},{8,9},{9,10},{10,1... | collective-permute-start | bytes 393224 | tf_op jit(solution)/shard_map/ppermute | solution.py:18
  64.5 0.9 collective-permute-done.1
  67.3 4.2 %scatter_fusion = f32[3,8,32,256]{3,2,1,0:T(8,128)S(1)} fusion(f32[3,8,32,256]{3,2,1,0:T(8,128)S(1)} %maximum_subtract_fusion, s32[48]{0:T(128)S(1)} %fusion.59, f32[48]{0:T(128)S(1)} %reshape.207), kind=kCustom, calls=%fused_computation.1 | custom fusion | flops 48 | bytes 1344 | tf_op jit(solution)/shard_map/scatter-add | solution.py:126
  71.5 1.7 %fusion.18 = (f32[1,8,32,256]{3,2,1,0:T(8,128)S(1)}, f32[1,8,32,256]{3,2,1,0:T(8,128)S(1)}, f32[1,8,32,256]{3,2,1,0:T(8,128)S(1)}) fusion(f32[7,32,256]{2,1,0:T(8,128)} %get-tuple-element.28, f32[1,32,256]{2,1,0:T(8,128)S(1)} %get-tuple-element.61, f32[8,32,255]{2,1,0:T(8,128)} %bitcast.192, f32[3,8,32,256]{3,2,1,0:T(8,128)S(1)} %fusion.1, ...), kind=kLoop, calls=%fused_computation.43 | loop fusion | flops 720896 | bytes 3127296 | tf_op jit(solution)/shard_map/stack | solution.py:57
  73.5 1.8 %multiply_reduce_fusion = (f32[8,32,256]{2,1,0:T(8,128)S(1)}, f32[3,8,32,256]{3,2,1,0:T(8,128)}, f32[3,8,32,256]{3,2,1,0:T(8,128)}) fusion(f32[3,8,32,256]{3,2,1,0:T(8,128)S(1)} %copy-done, f32[3,8,32,256]{3,2,1,0:T(8,128)S(1)} %copy-done.1, f32[8,32,256]{2,1,0:T(8,128)S(1)} %scatter_fusion.1, f32[3,8,32,256]{3,2,1,0:T(8,128)S(1)} %copy-done.18, ...), kind=kLoop, calls=%fused_computation.15 | loop fusion | flops 3866624 | bytes 7340032 | tf_op jit(solution)/shard_map/reduce_sum | solution.py:135
  76.5 1.1 copy.22
  77.7 55.9 %reduce-scatter.2.cloned.1.call-done = f32[1,32,256]{2,1,0:T(8,128)} async-done(((f32[16,32,256]{2,1,0:T(8,128)}), f32[1,32,256]{2,1,0:T(8,128)}) %reduce-scatter.2.cloned.1.call-update) | async-done | bytes 32784 | tf_op jit(solution)/shard_map/reduce_scatter | solution.py:139
  133.6 1.0 convolution_bitcast_fusion.2
  134.7 0.9 convolution_bitcast_fusion.1
  (115 shorter events, 10.7 us)
Async XLA Ops:
  7.2 6.9 %copy-start = (f32[3,8,32,256]{3,2,1,0:T(8,128)S(1)}, f32[3,8,32,256]{3,2,1,0:T(8,128)}, u32[]{:S(2)}) copy-start(f32[3,8,32,256]{3,2,1,0:T(8,128)} %param.14) | copy-start | bytes 2359300
  7.2 126.4 %reduce-scatter.2.cloned.1.call-start = ((), (), s32[]{:S(2)}) async-start(), calls=%async_computation.1 | async-start | bytes 557056 | tf_op jit(solution)/shard_map/reduce_scatter | solution.py:139
  8.8 47.3 %collective-permute-start = (f32[4,32,256]{2,1,0:T(8,128)}, f32[4,32,256]{2,1,0:T(8,128)S(1)}, u32[]{:S(2)}, u32[]{:S(2)}) collective-permute-start(f32[4,32,256]{2,1,0:T(8,128)} %pad_maximum_fusion), channel_id=1, source_target_pairs={{1,0},{2,1},{3,2},{4,3},{5,4},{6,5},{7,6},{8,7},{9,8},{10,9},{11,1... | collective-permute-start | bytes 393224 | tf_op jit(solution)/shard_map/ppermute | solution.py:18
  12.1 2.7 %copy-start.1 = (f32[3,8,32,256]{3,2,1,0:T(8,128)S(1)}, f32[3,8,32,256]{3,2,1,0:T(8,128)}, u32[]{:S(2)}) copy-start(f32[3,8,32,256]{3,2,1,0:T(8,128)} %param.18) | copy-start | bytes 2359300
  48.6 0.9 copy-start.11
  54.4 1.6 %copy-start.23 = (s32[48,1]{0,1:T(1,128)S(1)}, s32[48,1]{0,1:T(1,128)}, u32[]{:S(2)}) copy-start(s32[48,1]{0,1:T(1,128)} %reshape.193) | copy-start | bytes 580
  54.4 1.6 %copy-start.24 = (s32[48,1]{0,1:T(1,128)S(1)}, s32[48,1]{0,1:T(1,128)}, u32[]{:S(2)}) copy-start(s32[48,1]{0,1:T(1,128)} %tile.32) | copy-start | bytes 580
  54.4 1.6 %copy-start.25 = (s32[48,1]{0,1:T(1,128)S(1)}, s32[48,1]{0,1:T(1,128)}, u32[]{:S(2)}) copy-start(s32[48,1]{0,1:T(1,128)} %tile.30) | copy-start | bytes 580
  54.4 1.6 %copy-start.26 = (s32[48,1]{0,1:T(1,128)S(1)}, s32[48,1]{0,1:T(1,128)}, u32[]{:S(2)}) copy-start(s32[48,1]{0,1:T(1,128)} %tile.13) | copy-start | bytes 580
  54.4 1.7 %copy-start.14 = (f32[7,32,256]{2,1,0:T(8,128)S(1)}, f32[7,32,256]{2,1,0:T(8,128)}, u32[]{:S(2)}) copy-start(f32[7,32,256]{2,1,0:T(8,128)} %get-tuple-element.48) | copy-start | bytes 688132
  54.4 1.7 %copy-start.15 = (f32[7,32,256]{2,1,0:T(8,128)S(1)}, f32[7,32,256]{2,1,0:T(8,128)}, u32[]{:S(2)}) copy-start(f32[7,32,256]{2,1,0:T(8,128)} %get-tuple-element.49) | copy-start | bytes 688132
  56.1 1.0 copy-start.10
  57.0 1.1 copy-start.20
  58.3 13.2 %copy-start.2 = (f32[3,8,32,256]{3,2,1,0:T(8,128)}, f32[3,8,32,256]{3,2,1,0:T(8,128)S(1)}, u32[]{:S(2)}) copy-start(f32[3,8,32,256]{3,2,1,0:T(8,128)S(1)} %fusion.1) | copy-start | bytes 2359300
  59.2 1.0 copy-start.6
  59.2 1.2 copy-start.7
  59.2 1.4 copy-start.8
  59.2 1.5 %copy-start.9 = (f32[8,31,256]{2,1,0:T(8,128)S(1)}, f32[8,31,256]{2,1,0:T(8,128)}, u32[]{:S(2)}) copy-start(f32[8,31,256]{2,1,0:T(8,128)} %slice.273) | copy-start | bytes 761860
  59.2 1.5 %copy-start.12 = (f32[7,32,256]{2,1,0:T(8,128)S(1)}, f32[7,32,256]{2,1,0:T(8,128)}, u32[]{:S(2)}) copy-start(f32[7,32,256]{2,1,0:T(8,128)} %get-tuple-element.38) | copy-start | bytes 688132
  59.2 1.6 %copy-start.13 = (f32[7,32,256]{2,1,0:T(8,128)S(1)}, f32[7,32,256]{2,1,0:T(8,128)}, u32[]{:S(2)}) copy-start(f32[7,32,256]{2,1,0:T(8,128)} %get-tuple-element.39) | copy-start | bytes 688132
  60.8 1.1 copy-start.21
  62.1 3.4 %copy-start.3 = (f32[3,8,32,256]{3,2,1,0:T(8,128)}, f32[3,8,32,256]{3,2,1,0:T(8,128)S(1)}, u32[]{:S(2)}) copy-start(f32[3,8,32,256]{3,2,1,0:T(8,128)S(1)} %fusion) | copy-start | bytes 2359300
  62.2 3.2 %collective-permute-start.1 = (f32[4,32,256]{2,1,0:T(8,128)S(1)}, f32[4,32,256]{2,1,0:T(8,128)S(1)}, u32[]{:S(2)}, u32[]{:S(2)}) collective-permute-start(f32[4,32,256]{2,1,0:T(8,128)S(1)} %pad_maximum_fusion.1), channel_id=1, source_target_pairs={{0,1},{1,2},{2,3},{3,4},{4,5},{5,6},{6,7},{7,8},{8,9},{9,10},{10,1... | collective-permute-start | bytes 393224 | tf_op jit(solution)/shard_map/ppermute | solution.py:18
  65.4 1.0 copy-start.4
  65.5 1.2 copy-start.16
  65.5 1.4 %copy-start.17 = (f32[3,8,32,256]{3,2,1,0:T(8,128)S(1)}, f32[3,8,32,256]{3,2,1,0:T(8,128)}, u32[]{:S(2)}) copy-start(f32[3,8,32,256]{3,2,1,0:T(8,128)} %param.17) | copy-start | bytes 2359300
  71.5 1.8 %copy-start.5 = (f32[8,32,256]{2,1,0:T(8,128)S(1)}, f32[8,32,256]{2,1,0:T(8,128)}, u32[]{:S(2)}) copy-start(f32[8,32,256]{2,1,0:T(8,128)} %get-tuple-element.58) | copy-start | bytes 786436
  71.5 1.8 %copy-start.18 = (f32[3,8,32,256]{3,2,1,0:T(8,128)S(1)}, f32[3,8,32,256]{3,2,1,0:T(8,128)}, u32[]{:S(2)}) copy-start(f32[3,8,32,256]{3,2,1,0:T(8,128)} %param.20) | copy-start | bytes 2359300
  71.5 1.9 %copy-start.19 = (f32[3,8,32,256]{3,2,1,0:T(8,128)S(1)}, f32[3,8,32,256]{3,2,1,0:T(8,128)}, u32[]{:S(2)}) copy-start(f32[3,8,32,256]{3,2,1,0:T(8,128)} %param.21) | copy-start | bytes 2359300
  71.5 2.0 %copy-start.22 = (f32[8,32,256]{2,1,0:T(8,128)S(1)}, f32[8,32,256]{2,1,0:T(8,128)}, u32[]{:S(2)}) copy-start(f32[8,32,256]{2,1,0:T(8,128)} %get-tuple-element.57) | copy-start | bytes 786436
  77.6 56.0 %copy-start.34 = (f32[32]{0:T(128)S(1)}, f32[32]{0:T(128)}, u32[]{:S(2)}) copy-start(f32[32]{0:T(128)} %convert_reduce_fusion.1) | copy-start | bytes 388
  77.6 57.0 %copy-start.37 = (f32[256]{0:T(256)S(1)}, f32[256]{0:T(256)}, u32[]{:S(2)}) copy-start(f32[256]{0:T(256)} %convert_reduce_fusion) | copy-start | bytes 3076
  (9 other events, 5.9 us)
Sparse Core Ops, SparseCore 0:
  77.8 55.7 reduce-scatter.1
where the time goes:
time: 143 us; the launch traced here: 142 us
  waiting for transfers between devices  56.9 us (40%)
  blocking collectives  25.4 us (18%)
  local copies, waits for them, and re-layouts  22.6 us (16%)
  between operations  15.9 us (11%)
  other arithmetic  13.9 us (10%)
  matrix products  4.26 us (3%)
  starting transfers between devices  3.57 us (2%)
    reduce_scatter x1, waiting for transfers between devices, body(): lax.psum_scatter(returned, 'gx', scatter_dimension=0, tiled=True)  55.9 us
    all_gather x1, blocking collectives, body(): gathered = lax.all_gather(design, 'gx', axis=0, tiled=True)  25.4 us
    unnamed x76, local copies, waits for them, and re-layouts  7.77 us
    scatter-add x1, other arithmetic, body(): drive = jnp.zeros((3, depth, width_x, width_y), jnp.float32).at[comp, jnp...  4.22 us
    slice x8, local copies, waits for them, and re-layouts, ahead(): rest = lax.slice_in_dim(field, 1, count, axis=axis)  4.17 us
    ppermute x2, starting transfers between devices, passed_along(): return lax.ppermute(block, axis, route)  3.53 us
  transfers between devices with their start and end apart: 3, of which 2 were waited for; matrix products, arithmetic and copies ran while one was open for 12% of the time, Pallas kernels for 0%

commit v1 on v0

--- a/solution.py
+++ b/solution.py
@@ -108,7 +108,16 @@
     )
     hf = update_h(e_forward, h_forward, upper[0:2])
     ha = update_h(e_adjoint, h_adjoint, upper[2:4])
-    gathered = lax.all_gather(design, "gx", axis=0, tiled=True)
+    ways = lax.axis_size("gx")
+    up = [(d, (d + 1) % ways) for d in range(ways)]
+    down = [(d, (d - 1) % ways) for d in range(ways)]
+    earlier, later = ([design], [design])
+    for _ in range(ways // 2):
+        earlier.append(lax.ppermute(earlier[-1], "gx", up))
+    for _ in range((ways - 1) // 2):
+        later.append(lax.ppermute(later[-1], "gx", down))
+    line = jnp.concatenate([*earlier[::-1], *later[1:]], axis=0)
+    gathered = jnp.roll(line, (lax.axis_index("gx") - ways // 2) * design.shape[0], axis=0)
     slab = gathered.shape[0]
     planes = index * depth + jnp.arange(depth, dtype=jnp.int32) - start
     valid = ((planes >= 0) & (planes < slab)).astype(jnp.float32)

time: 143 us -> 170 us (1.19)
  starting transfers between devices: 3.57 us -> 35.1 us
  blocking collectives: 25.4 us -> 0 us
  local copies, waits for them, and re-layouts: 22.6 us -> 33.6 us
  waiting for transfers between devices: 56.9 us -> 64.4 us
    ppermute x0 -> x15, starting transfers between devices: none -> 31.7 us  [the longest x7 30 us: body(): later.append(lax.ppermute(later[-1], 'gx', down))]
    all_gather x1 -> x0, blocking collectives: 25.4 us -> none  [body(): gathered = lax.all_gather(design, 'gx', axis=0, tiled=True)]
    ppermute x0 -> x15, waiting for transfers between devices: none -> 10.3 us  [the longest x8 10.2 us: body(): earlier.append(lax.ppermute(earlier[-1], 'gx', up))]
    unnamed x76 -> x117, local copies, waits for them, and re-layouts: 7.77 us -> 15.4 us
    reduce_scatter x1, waiting for transfers between devices: 55.9 us -> 54.1 us  [body(): lax.psum_scatter(returned, 'gx', scatter_dimension=0, tiled=True)]
    gather x1, local copies, waits for them, and re-layouts: 0.56 us -> 2.3 us  [body(): jnp.take(gathered, jnp.clip(planes, 0, slab - 1), axis=0)]
  transfers between devices with their start and end apart: 3 -> 18, of which waited for: 2 -> 7; matrix products, arithmetic and copies ran while one was open for 12% -> 18% of each run, Pallas kernels for 0% -> 0%
where the time goes in v1:
time: 170 us; the launch traced here: 168 us
  waiting for transfers between devices  64.4 us (38%)
  starting transfers between devices  35.1 us (21%)
  local copies, waits for them, and re-layouts  33.6 us (20%)
  between operations  16 us (9%)
  other arithmetic  14 us (8%)
  matrix products  5.13 us (3%)
    reduce_scatter x1, waiting for transfers between devices, body(): lax.psum_scatter(returned, 'gx', scatter_dimension=0, tiled=True)  54.1 us
    ppermute x7, starting transfers between devices, body(): later.append(lax.ppermute(later[-1], 'gx', down))  30 us
    unnamed x117, local copies, waits for them, and re-layouts  15.4 us
    ppermute x8, waiting for transfers between devices, body(): earlier.append(lax.ppermute(earlier[-1], 'gx', up))  10.2 us
    scatter-add x1, other arithmetic, body(): drive = jnp.zeros((3, depth, width_x, width_y), jnp.float32).at[comp, jnp...  4.22 us
    slice x8, local copies, waits for them, and re-layouts, ahead(): rest = lax.slice_in_dim(field, 1, count, axis=axis)  4.16 us
  transfers between devices with their start and end apart: 18, of which 7 were waited for; matrix products, arithmetic and copies ran while one was open for 18% of the time, Pallas kernels for 0%

profile of v1, /device:TPU:0, one launch (start us, length us, event | category | flops | bytes accessed | tf_op | source)
XLA Modules:
  0.0 168.3 jit_solution(18215383341191028139)
XLA Ops:
  7.7 5.1 %collective-permute-start.8 = (f32[1,32,256]{2,1,0:T(8,128)}, f32[1,32,256]{2,1,0:T(8,128)S(1)}, u32[]{:S(2)}, u32[]{:S(2)}) collective-permute-start(f32[1,32,256]{2,1,0:T(8,128)} %param.22), channel_id=1, source_target_pairs={{0,15},{1,0},{2,1},{3,2},{4,3},{5,4},{6,5},{7,6},{8,7},{9,8},{10,9... | collective-permute-start | bytes 98312 | tf_op jit(solution)/shard_map/ppermute | solution.py:118
  14.3 1.4 collective-permute-start.15
  15.7 1.2 slice_bitcast_fusion.11
  23.3 1.1 collective-permute-start.1
  24.4 3.3 %collective-permute-start.9 = (f32[1,32,256]{2,1,0:T(8,128)S(1)}, f32[1,32,256]{2,1,0:T(8,128)}, u32[]{:S(2)}, u32[]{:S(2)}) collective-permute-start(f32[1,32,256]{2,1,0:T(8,128)S(1)} %collective-permute-done.8), channel_id=1, source_target_pairs={{0,15},{1,0},{2,1},{3,2},{4,3},{5,4},{6,5},{7,6},{8,7},{9,8},{10,9... | collective-permute-start | bytes 98312 | tf_op jit(solution)/shard_map/ppermute | solution.py:118
  27.8 1.7 %collective-permute-done.1 = f32[1,32,256]{2,1,0:T(8,128)} collective-permute-done((f32[1,32,256]{2,1,0:T(8,128)S(1)}, f32[1,32,256]{2,1,0:T(8,128)}, u32[]{:S(2)}, u32[]{:S(2)}) %collective-permute-start.1) | collective-permute-done | bytes 32800 | tf_op jit(solution)/shard_map/ppermute | solution.py:116
  29.5 4.4 %collective-permute-start.10 = (f32[1,32,256]{2,1,0:T(8,128)}, f32[1,32,256]{2,1,0:T(8,128)}, u32[]{:S(2)}, u32[]{:S(2)}) collective-permute-start(f32[1,32,256]{2,1,0:T(8,128)} %collective-permute-done.9), channel_id=1, source_target_pairs={{0,15},{1,0},{2,1},{3,2},{4,3},{5,4},{6,5},{7,6},{8,7},{9,8},{10,9... | collective-permute-start | bytes 98312 | tf_op jit(solution)/shard_map/ppermute | solution.py:118
  34.1 0.8 slice.280
  40.2 1.6 scatter_fusion.1
  42.6 4.4 %collective-permute-start.11 = (f32[1,32,256]{2,1,0:T(8,128)}, f32[1,32,256]{2,1,0:T(8,128)S(1)}, u32[]{:S(2)}, u32[]{:S(2)}) collective-permute-start(f32[1,32,256]{2,1,0:T(8,128)} %collective-permute-done.10), channel_id=1, source_target_pairs={{0,15},{1,0},{2,1},{3,2},{4,3},{5,4},{6,5},{7,6},{8,7},{9,8},{10,9... | collective-permute-start | bytes 98312 | tf_op jit(solution)/shard_map/ppermute | solution.py:118
  47.3 0.9 copy-done.25
  48.4 0.9 slice_bitcast_fusion.5
  50.5 0.9 copy-done.26
  51.5 1.0 slice_bitcast_fusion.2
  54.1 5.2 %collective-permute-done.4 = f32[1,32,256]{2,1,0:T(8,128)S(1)} collective-permute-done((f32[1,32,256]{2,1,0:T(8,128)S(1)}, f32[1,32,256]{2,1,0:T(8,128)S(1)}, u32[]{:S(2)}, u32[]{:S(2)}) %collective-permute-start.4) | collective-permute-done | bytes 32800 | tf_op jit(solution)/shard_map/ppermute | solution.py:116
  59.4 4.5 %collective-permute-start.12 = (f32[1,32,256]{2,1,0:T(8,128)S(1)}, f32[1,32,256]{2,1,0:T(8,128)S(1)}, u32[]{:S(2)}, u32[]{:S(2)}) collective-permute-start(f32[1,32,256]{2,1,0:T(8,128)S(1)} %collective-permute-done.11), channel_id=1, source_target_pairs={{0,15},{1,0},{2,1},{3,2},{4,3},{5,4},{6,5},{7,6},{8,7},{9,8},{10,9... | collective-permute-start | bytes 98312 | tf_op jit(solution)/shard_map/ppermute | solution.py:118
  63.9 1.5 collective-permute-done.5
  65.5 4.4 %collective-permute-start.13 = (f32[1,32,256]{2,1,0:T(8,128)S(1)}, f32[1,32,256]{2,1,0:T(8,128)S(1)}, u32[]{:S(2)}, u32[]{:S(2)}) collective-permute-start(f32[1,32,256]{2,1,0:T(8,128)S(1)} %collective-permute-done.12), channel_id=1, source_target_pairs={{0,15},{1,0},{2,1},{3,2},{4,3},{5,4},{6,5},{7,6},{8,7},{9,8},{10,9... | collective-permute-start | bytes 98312 | tf_op jit(solution)/shard_map/ppermute | solution.py:118
  69.9 1.5 collective-permute-done.6
  71.5 1.9 %collective-permute-start.16 = (f32[4,32,256]{2,1,0:T(8,128)S(1)}, f32[4,32,256]{2,1,0:T(8,128)}, u32[]{:S(2)}, u32[]{:S(2)}) collective-permute-start(f32[4,32,256]{2,1,0:T(8,128)S(1)} %pad_maximum_fusion.1), channel_id=1, source_target_pairs={{0,1},{1,2},{2,3},{3,4},{4,5},{5,6},{6,7},{7,8},{8,9},{9,10},{10,1... | collective-permute-start | bytes 393224 | tf_op jit(solution)/shard_map/ppermute | solution.py:18
  73.4 3.9 %collective-permute-start.14 = (f32[1,32,256]{2,1,0:T(8,128)S(1)}, f32[1,32,256]{2,1,0:T(8,128)S(1)}, u32[]{:S(2)}, u32[]{:S(2)}) collective-permute-start(f32[1,32,256]{2,1,0:T(8,128)S(1)} %collective-permute-done.13), channel_id=1, source_target_pairs={{0,15},{1,0},{2,1},{3,2},{4,3},{5,4},{6,5},{7,6},{8,7},{9,8},{10,9... | collective-permute-start | bytes 98312 | tf_op jit(solution)/shard_map/ppermute | solution.py:118
  86.2 2.3 %gather_fusion = f32[8,32,256]{2,1,0:T(8,128)} fusion(f32[16,32,256]{2,1,0:T(8,128)} %constant_dynamic-slice_fusion, s32[1024]{0:T(1024)S(1)} %pad_clamp_fusion), kind=kCustom, calls=%fused_computation | custom fusion | bytes 524320 | tf_op jit(solution)/shard_map/jit(_take)/gather | solution.py:124
  89.1 1.4 convolution_bitcast_fusion
  90.6 1.2 add_divide_fusion
  91.8 0.9 fusion.68
  94.9 4.2 %scatter_fusion = f32[3,8,32,256]{3,2,1,0:T(8,128)S(1)} fusion(f32[3,8,32,256]{3,2,1,0:T(8,128)S(1)} %maximum_subtract_fusion, s32[48]{0:T(128)S(1)} %fusion.59, f32[48]{0:T(128)S(1)} %copy-done.33), kind=kCustom, calls=%fused_computation.1 | custom fusion | flops 48 | bytes 1344 | tf_op jit(solution)/shard_map/scatter-add | solution.py:135
  99.2 1.8 %fusion.18 = (f32[1,8,32,256]{3,2,1,0:T(8,128)S(1)}, f32[1,8,32,256]{3,2,1,0:T(8,128)S(1)}, f32[1,8,32,256]{3,2,1,0:T(8,128)S(1)}) fusion(f32[7,32,256]{2,1,0:T(8,128)} %get-tuple-element.28, f32[1,32,256]{2,1,0:T(8,128)S(1)} %get-tuple-element.61, f32[8,32,255]{2,1,0:T(8,128)} %bitcast.194, f32[3,8,32,256]{3,2,1,0:T(8,128)S(1)} %fusion.1, ...), kind=kLoop, calls=%fused_computation.43 | loop fusion | flops 720896 | bytes 3127296 | tf_op jit(solution)/shard_map/stack | solution.py:57
  101.1 1.8 %multiply_reduce_fusion = (f32[8,32,256]{2,1,0:T(8,128)S(1)}, f32[3,8,32,256]{3,2,1,0:T(8,128)}, f32[3,8,32,256]{3,2,1,0:T(8,128)}) fusion(f32[3,8,32,256]{3,2,1,0:T(8,128)S(1)} %copy-done, f32[3,8,32,256]{3,2,1,0:T(8,128)S(1)} %copy-done.1, f32[8,32,256]{2,1,0:T(8,128)S(1)} %scatter_fusion.1, f32[3,8,32,256]{3,2,1,0:T(8,128)S(1)} %copy-done.23, ...), kind=kLoop, calls=%fused_computation.15 | loop fusion | flops 3866624 | bytes 7340032 | tf_op jit(solution)/shard_map/reduce_sum | solution.py:144
  104.2 1.1 copy.22
  105.3 54.1 %reduce-scatter.2.cloned.1.call-done = f32[1,32,256]{2,1,0:T(8,128)} async-done(((f32[16,32,256]{2,1,0:T(8,128)}), f32[1,32,256]{2,1,0:T(8,128)}) %reduce-scatter.2.cloned.1.call-update) | async-done | bytes 32784 | tf_op jit(solution)/shard_map/reduce_scatter | solution.py:148
  159.5 1.0 convolution_bitcast_fusion.2
  160.5 0.9 convolution_bitcast_fusion.1
  (187 shorter events, 29.6 us)
Async XLA Ops:
  7.2 152.3 %reduce-scatter.2.cloned.1.call-start = ((), (), s32[]{:S(2)}) async-start(), calls=%async_computation.1 | async-start | bytes 557056 | tf_op jit(solution)/shard_map/reduce_scatter | solution.py:148
  7.2 16.1 %collective-permute-start = (f32[1,32,256]{2,1,0:T(8,128)}, f32[1,32,256]{2,1,0:T(8,128)S(1)}, u32[]{:S(2)}, u32[]{:S(2)}) collective-permute-start(f32[1,32,256]{2,1,0:T(8,128)} %param.22), channel_id=1, source_target_pairs={{0,1},{1,2},{2,3},{3,4},{4,5},{5,6},{6,7},{7,8},{8,9},{9,10},{10,1... | collective-permute-start | bytes 98312 | tf_op jit(solution)/shard_map/ppermute | solution.py:116
  7.7 16.7 %collective-permute-start.8 = (f32[1,32,256]{2,1,0:T(8,128)}, f32[1,32,256]{2,1,0:T(8,128)S(1)}, u32[]{:S(2)}, u32[]{:S(2)}) collective-permute-start(f32[1,32,256]{2,1,0:T(8,128)} %param.22), channel_id=1, source_target_pairs={{0,15},{1,0},{2,1},{3,2},{4,3},{5,4},{6,5},{7,6},{8,7},{9,8},{10,9... | collective-permute-start | bytes 98312 | tf_op jit(solution)/shard_map/ppermute | solution.py:118
  14.3 2.6 %copy-start = (f32[3,8,32,256]{3,2,1,0:T(8,128)S(1)}, f32[3,8,32,256]{3,2,1,0:T(8,128)}, u32[]{:S(2)}) copy-start(f32[3,8,32,256]{3,2,1,0:T(8,128)} %param.14) | copy-start | bytes 2359300
  14.3 32.8 %collective-permute-start.15 = (f32[4,32,256]{2,1,0:T(8,128)}, f32[4,32,256]{2,1,0:T(8,128)S(1)}, u32[]{:S(2)}, u32[]{:S(2)}) collective-permute-start(f32[4,32,256]{2,1,0:T(8,128)} %pad_maximum_fusion), channel_id=1, source_target_pairs={{1,0},{2,1},{3,2},{4,3},{5,4},{6,5},{7,6},{8,7},{9,8},{10,9},{11,1... | collective-permute-start | bytes 393224 | tf_op jit(solution)/shard_map/ppermute | solution.py:18
  23.3 10.6 %copy-start.31 = (f32[1,32,256]{2,1,0:T(8,128)}, f32[1,32,256]{2,1,0:T(8,128)S(1)}, u32[]{:S(2)}) copy-start(f32[1,32,256]{2,1,0:T(8,128)S(1)} %collective-permute-done) | copy-start | bytes 98308
  23.3 6.1 %collective-permute-start.1 = (f32[1,32,256]{2,1,0:T(8,128)S(1)}, f32[1,32,256]{2,1,0:T(8,128)}, u32[]{:S(2)}, u32[]{:S(2)}) collective-permute-start(f32[1,32,256]{2,1,0:T(8,128)S(1)} %collective-permute-done), channel_id=1, source_target_pairs={{0,1},{1,2},{2,3},{3,4},{4,5},{5,6},{6,7},{7,8},{8,9},{9,10},{10,1... | collective-permute-start | bytes 98312 | tf_op jit(solution)/shard_map/ppermute | solution.py:116
  24.4 9.5 %copy-start.29 = (f32[1,32,256]{2,1,0:T(8,128)}, f32[1,32,256]{2,1,0:T(8,128)S(1)}, u32[]{:S(2)}) copy-start(f32[1,32,256]{2,1,0:T(8,128)S(1)} %collective-permute-done.8) | copy-start | bytes 98308
  24.4 5.0 %collective-permute-start.9 = (f32[1,32,256]{2,1,0:T(8,128)S(1)}, f32[1,32,256]{2,1,0:T(8,128)}, u32[]{:S(2)}, u32[]{:S(2)}) collective-permute-start(f32[1,32,256]{2,1,0:T(8,128)S(1)} %collective-permute-done.8), channel_id=1, source_target_pairs={{0,15},{1,0},{2,1},{3,2},{4,3},{5,4},{6,5},{7,6},{8,7},{9,8},{10,9... | collective-permute-start | bytes 98312 | tf_op jit(solution)/shard_map/ppermute | solution.py:118
  29.5 13.2 %collective-permute-start.2 = (f32[1,32,256]{2,1,0:T(8,128)}, f32[1,32,256]{2,1,0:T(8,128)}, u32[]{:S(2)}, u32[]{:S(2)}) collective-permute-start(f32[1,32,256]{2,1,0:T(8,128)} %collective-permute-done.1), channel_id=1, source_target_pairs={{0,1},{1,2},{2,3},{3,4},{4,5},{5,6},{6,7},{7,8},{8,9},{9,10},{10,1... | collective-permute-start | bytes 98312 | tf_op jit(solution)/shard_map/ppermute | solution.py:116
  29.5 13.2 %collective-permute-start.10 = (f32[1,32,256]{2,1,0:T(8,128)}, f32[1,32,256]{2,1,0:T(8,128)}, u32[]{:S(2)}, u32[]{:S(2)}) collective-permute-start(f32[1,32,256]{2,1,0:T(8,128)} %collective-permute-done.9), channel_id=1, source_target_pairs={{0,15},{1,0},{2,1},{3,2},{4,3},{5,4},{6,5},{7,6},{8,7},{9,8},{10,9... | collective-permute-start | bytes 98312 | tf_op jit(solution)/shard_map/ppermute | solution.py:118
  40.2 6.9 %copy-start.17 = (f32[7,32,256]{2,1,0:T(8,128)S(1)}, f32[7,32,256]{2,1,0:T(8,128)}, u32[]{:S(2)}) copy-start(f32[7,32,256]{2,1,0:T(8,128)} %get-tuple-element.38) | copy-start | bytes 688132
  40.2 6.9 %copy-start.18 = (f32[7,32,256]{2,1,0:T(8,128)S(1)}, f32[7,32,256]{2,1,0:T(8,128)}, u32[]{:S(2)}) copy-start(f32[7,32,256]{2,1,0:T(8,128)} %get-tuple-element.39) | copy-start | bytes 688132
  41.7 5.4 %copy-start.11 = (f32[8,32,255]{2,1,0:T(8,128)S(1)}, f32[8,32,255]{2,1,0:T(8,128)}, u32[]{:S(2)}) copy-start(f32[8,32,255]{2,1,0:T(8,128)} %slice.274) | copy-start | bytes 783364
  42.6 10.7 %collective-permute-start.3 = (f32[1,32,256]{2,1,0:T(8,128)}, f32[1,32,256]{2,1,0:T(8,128)S(1)}, u32[]{:S(2)}, u32[]{:S(2)}) collective-permute-start(f32[1,32,256]{2,1,0:T(8,128)} %collective-permute-done.2), channel_id=1, source_target_pairs={{0,1},{1,2},{2,3},{3,4},{4,5},{5,6},{6,7},{7,8},{8,9},{9,10},{10,1... | collective-permute-start | bytes 98312 | tf_op jit(solution)/shard_map/ppermute | solution.py:116
  42.6 16.8 %collective-permute-start.11 = (f32[1,32,256]{2,1,0:T(8,128)}, f32[1,32,256]{2,1,0:T(8,128)S(1)}, u32[]{:S(2)}, u32[]{:S(2)}) collective-permute-start(f32[1,32,256]{2,1,0:T(8,128)} %collective-permute-done.10), channel_id=1, source_target_pairs={{0,15},{1,0},{2,1},{3,2},{4,3},{5,4},{6,5},{7,6},{8,7},{9,8},{10,9... | collective-permute-start | bytes 98312 | tf_op jit(solution)/shard_map/ppermute | solution.py:118
  48.4 44.4 %copy-start.2 = (f32[3,8,32,256]{3,2,1,0:T(8,128)}, f32[3,8,32,256]{3,2,1,0:T(8,128)S(1)}, u32[]{:S(2)}) copy-start(f32[3,8,32,256]{3,2,1,0:T(8,128)S(1)} %fusion) | copy-start | bytes 2359300
  51.5 47.6 %copy-start.3 = (f32[3,8,32,256]{3,2,1,0:T(8,128)}, f32[3,8,32,256]{3,2,1,0:T(8,128)S(1)}, u32[]{:S(2)}) copy-start(f32[3,8,32,256]{3,2,1,0:T(8,128)S(1)} %fusion.1) | copy-start | bytes 2359300
  53.3 6.0 %collective-permute-start.4 = (f32[1,32,256]{2,1,0:T(8,128)S(1)}, f32[1,32,256]{2,1,0:T(8,128)S(1)}, u32[]{:S(2)}, u32[]{:S(2)}) collective-permute-start(f32[1,32,256]{2,1,0:T(8,128)S(1)} %collective-permute-done.3), channel_id=1, source_target_pairs={{0,1},{1,2},{2,3},{3,4},{4,5},{5,6},{6,7},{7,8},{8,9},{9,10},{10,1... | collective-permute-start | bytes 98312 | tf_op jit(solution)/shard_map/ppermute | solution.py:116
  59.4 6.0 %collective-permute-start.5 = (f32[1,32,256]{2,1,0:T(8,128)S(1)}, f32[1,32,256]{2,1,0:T(8,128)S(1)}, u32[]{:S(2)}, u32[]{:S(2)}) collective-permute-start(f32[1,32,256]{2,1,0:T(8,128)S(1)} %collective-permute-done.4), channel_id=1, source_target_pairs={{0,1},{1,2},{2,3},{3,4},{4,5},{5,6},{6,7},{7,8},{8,9},{9,10},{10,1... | collective-permute-start | bytes 98312 | tf_op jit(solution)/shard_map/ppermute | solution.py:116
  59.4 6.1 %collective-permute-start.12 = (f32[1,32,256]{2,1,0:T(8,128)S(1)}, f32[1,32,256]{2,1,0:T(8,128)S(1)}, u32[]{:S(2)}, u32[]{:S(2)}) collective-permute-start(f32[1,32,256]{2,1,0:T(8,128)S(1)} %collective-permute-done.11), channel_id=1, source_target_pairs={{0,15},{1,0},{2,1},{3,2},{4,3},{5,4},{6,5},{7,6},{8,7},{9,8},{10,9... | collective-permute-start | bytes 98312 | tf_op jit(solution)/shard_map/ppermute | solution.py:118
  65.4 6.0 %collective-permute-start.6 = (f32[1,32,256]{2,1,0:T(8,128)S(1)}, f32[1,32,256]{2,1,0:T(8,128)S(1)}, u32[]{:S(2)}, u32[]{:S(2)}) collective-permute-start(f32[1,32,256]{2,1,0:T(8,128)S(1)} %collective-permute-done.5), channel_id=1, source_target_pairs={{0,1},{1,2},{2,3},{3,4},{4,5},{5,6},{6,7},{7,8},{8,9},{9,10},{10,1... | collective-permute-start | bytes 98312 | tf_op jit(solution)/shard_map/ppermute | solution.py:116
  65.5 7.9 %collective-permute-start.13 = (f32[1,32,256]{2,1,0:T(8,128)S(1)}, f32[1,32,256]{2,1,0:T(8,128)S(1)}, u32[]{:S(2)}, u32[]{:S(2)}) collective-permute-start(f32[1,32,256]{2,1,0:T(8,128)S(1)} %collective-permute-done.12), channel_id=1, source_target_pairs={{0,15},{1,0},{2,1},{3,2},{4,3},{5,4},{6,5},{7,6},{8,7},{9,8},{10,9... | collective-permute-start | bytes 98312 | tf_op jit(solution)/shard_map/ppermute | solution.py:118
  71.4 6.0 %collective-permute-start.7 = (f32[1,32,256]{2,1,0:T(8,128)S(1)}, f32[1,32,256]{2,1,0:T(8,128)S(1)}, u32[]{:S(2)}, u32[]{:S(2)}) collective-permute-start(f32[1,32,256]{2,1,0:T(8,128)S(1)} %collective-permute-done.6), channel_id=1, source_target_pairs={{0,1},{1,2},{2,3},{3,4},{4,5},{5,6},{6,7},{7,8},{8,9},{9,10},{10,1... | collective-permute-start | bytes 98312 | tf_op jit(solution)/shard_map/ppermute | solution.py:116
  71.5 20.3 %collective-permute-start.16 = (f32[4,32,256]{2,1,0:T(8,128)S(1)}, f32[4,32,256]{2,1,0:T(8,128)}, u32[]{:S(2)}, u32[]{:S(2)}) collective-permute-start(f32[4,32,256]{2,1,0:T(8,128)S(1)} %pad_maximum_fusion.1), channel_id=1, source_target_pairs={{0,1},{1,2},{2,3},{3,4},{4,5},{5,6},{6,7},{7,8},{8,9},{9,10},{10,1... | collective-permute-start | bytes 393224 | tf_op jit(solution)/shard_map/ppermute | solution.py:18
  73.4 8.7 %collective-permute-start.14 = (f32[1,32,256]{2,1,0:T(8,128)S(1)}, f32[1,32,256]{2,1,0:T(8,128)S(1)}, u32[]{:S(2)}, u32[]{:S(2)}) collective-permute-start(f32[1,32,256]{2,1,0:T(8,128)S(1)} %collective-permute-done.13), channel_id=1, source_target_pairs={{0,15},{1,0},{2,1},{3,2},{4,3},{5,4},{6,5},{7,6},{8,7},{9,8},{10,9... | collective-permute-start | bytes 98312 | tf_op jit(solution)/shard_map/ppermute | solution.py:118
  90.5 2.2 %copy-start.12 = (f32[8,32,256]{2,1,0:T(8,128)S(1)}, f32[8,32,256]{2,1,0:T(8,128)}, u32[]{:S(2)}) copy-start(f32[8,32,256]{2,1,0:T(8,128)} %get-tuple-element.23) | copy-start | bytes 786436
  90.5 2.2 %copy-start.13 = (f32[8,32,256]{2,1,0:T(8,128)S(1)}, f32[8,32,256]{2,1,0:T(8,128)}, u32[]{:S(2)}) copy-start(f32[8,32,256]{2,1,0:T(8,128)} %get-tuple-element.24) | copy-start | bytes 786436
  90.5 2.2 %copy-start.19 = (f32[7,32,256]{2,1,0:T(8,128)S(1)}, f32[7,32,256]{2,1,0:T(8,128)}, u32[]{:S(2)}) copy-start(f32[7,32,256]{2,1,0:T(8,128)} %get-tuple-element.20) | copy-start | bytes 688132
  90.6 2.2 %copy-start.20 = (f32[7,32,256]{2,1,0:T(8,128)S(1)}, f32[7,32,256]{2,1,0:T(8,128)}, u32[]{:S(2)}) copy-start(f32[7,32,256]{2,1,0:T(8,128)} %get-tuple-element.21) | copy-start | bytes 688132
  99.1 1.9 %copy-start.24 = (f32[3,8,32,256]{3,2,1,0:T(8,128)S(1)}, f32[3,8,32,256]{3,2,1,0:T(8,128)}, u32[]{:S(2)}) copy-start(f32[3,8,32,256]{3,2,1,0:T(8,128)} %param.21) | copy-start | bytes 2359300
  99.2 2.0 %copy-start.27 = (f32[8,32,256]{2,1,0:T(8,128)S(1)}, f32[8,32,256]{2,1,0:T(8,128)}, u32[]{:S(2)}) copy-start(f32[8,32,256]{2,1,0:T(8,128)} %get-tuple-element.57) | copy-start | bytes 786436
  (29 other events, 33.5 us)
Sparse Core Ops, SparseCore 0:
  105.4 53.9 reduce-scatter.1
